TPU v7x, 256 devices: a whole 4x4x8 slice. The times are simulated.
256 devices in a mesh: day: 8 (over x, core), row: 32 (over y, z).
Axes of the slice: x: 4, y: 4, z: 8, core: 2. Of those that a mesh axis runs over, the one named last changes fastest.
Arguments:
- features: bfloat16 [8, 768, 16, 128, 128], P('day', 'row'), may hold values from -6 to 6
- blocks: int32 [8, 768, 16], P('day', 'row'), may hold values from 0 to 255, as said below
- labels: int32 [8, 768, 128], P('day', 'row'), may hold values from 0 to 15
- coef: float32 [8, 16, 32768], P('day', None, 'row'), may hold values from -0.125 to 0.125
- direction: float32 [8, 16, 32768], P('day', None, 'row'), may hold values from -0.125 to 0.125
- prior: float32 [32768], P('row'), may hold values from 100 to 3000
Outputs:
- gradient: float32 [8, 16, 32768], P('day', None, 'row')
- hess_dir: float32 [8, 16, 32768], P('day', None, 'row')
Inputs may be any that keep to these rules, and one draw needn't show every extreme that they name: `blocks`: within one row tile the 16 block numbers are distinct.
All inputs are finite; a program needn't handle non-finite values.
Results may differ from a plain program's by a relative error of at most 0.0003.
Values may be sent and summed in bfloat16 or wider, within the bound.
No kernel may reach another device: no remote copies, remote signals or barrier semaphores. Data moves between devices by JAX's collectives and lax.ppermute only.
A program may use at most 64 MiB of HBM per device.

v0:
```python
import jax
import jax.numpy as jnp
from jax import lax
from jax.sharding import Mesh
from jax.sharding import PartitionSpec as P

ROW = ("row_0", "row_1")


def copy_for_each(value, axis):
    copies = jnp.broadcast_to(value, (lax.axis_size(axis), *value.shape))
    return lax.all_to_all(copies, axis, split_axis=0, concat_axis=0, tiled=True)


def extended(cells, sides, width):
    for axis, dim in sides:
        count = lax.axis_size(axis)
        ends = count - 1
        head = lax.slice_in_dim(cells, 0, width, axis=dim)
        tail = lax.slice_in_dim(cells, cells.shape[dim] - width, cells.shape[dim], axis=dim)
        cells = jnp.concatenate(
            [
                lax.ppermute(tail, axis, [(i, (i + 1) % count) for i in range(ends)]),
                cells,
                lax.ppermute(head, axis, [((i + 1) % count, i) for i in range(ends)]),
            ],
            axis=dim,
        )
    return cells


def scatter_axes(value, axes, dim):
    if not axes:
        return value
    nearer = lax.psum_scatter(value, axes[0], scatter_dimension=dim, tiled=True)
    return scatter_axes(nearer, axes[1:], dim)


def on_device(features, blocks, labels, coef, direction, prior):
    arms = coef.shape[1]
    width = features.shape[-1]
    coef_pair = jnp.concatenate([coef[0], direction[0]], axis=0).astype(jnp.bfloat16)
    local_blk = coef_pair.shape[1] // width
    by_block = coef_pair.reshape(2 * arms, local_blk, width).transpose(1, 0, 2)
    coef_table = lax.all_gather(by_block, "row_1", axis=0, tiled=True)
    coef_table = lax.all_gather(coef_table, "row_0", axis=0, tiled=True)
    nblk = coef_table.shape[0]
    both = jnp.concatenate([coef, direction], axis=1)
    neighbours = extended(both, (("day", 0),), 1)
    blks = blocks[0]
    selected = coef_table[blks]
    feats = features[0]
    logits_dir = jnp.einsum("tari,taki->tkr", feats, selected, preferred_element_type=jnp.float32)
    logits = logits_dir[:, :arms]
    lin_dir = logits_dir[:, arms:]
    expo = jnp.exp(logits)
    probs = expo / jnp.sum(expo, axis=1, keepdims=True)
    onehot = (labels[0][:, None, :] == jnp.arange(arms, dtype=jnp.int32)[None, :, None]).astype(
        jnp.float32
    )
    resid = probs - onehot
    hrow = probs * lin_dir - probs * jnp.sum(probs * lin_dir, axis=1, keepdims=True)
    both_low = jnp.concatenate([resid, hrow], axis=1).astype(jnp.bfloat16)
    contrib = jnp.einsum("tari,tkr->taki", feats, both_low, preferred_element_type=jnp.float32)
    contrib = contrib.reshape(-1, 2 * arms * width)
    top = lax.reduce_precision(contrib, exponent_bits=8, mantissa_bits=7)
    hi = top.astype(jnp.bfloat16)
    lo = (contrib - top).astype(jnp.bfloat16)
    outer = lax.axis_size("row_0")
    inner = lax.axis_size("row_1")
    order = jnp.arange(nblk, dtype=jnp.int32).reshape(outer, inner, -1).transpose(1, 0, 2)
    place = (order.reshape(-1)[:, None] == blks.reshape(-1)[None, :]).astype(jnp.bfloat16)
    split = jnp.einsum(
        "bp,jpc->jbc", place, jnp.stack([hi, lo], axis=0), preferred_element_type=jnp.float32
    )
    partial_terms = (split[0] + split[1]).reshape(nblk, 2 * arms, width)
    owned = lax.psum_scatter(partial_terms, "row_1", scatter_dimension=0, tiled=True)
    owned = lax.psum_scatter(owned, "row_0", scatter_dimension=0, tiled=True)
    owned = owned.transpose(1, 0, 2).reshape(2 * arms, -1)
    day_index = lax.axis_index("day")
    ndays = lax.axis_size("day")
    links = (day_index > 0).astype(jnp.float32) + (day_index < ndays - 1).astype(jnp.float32)
    coupling = links * neighbours[1] - neighbours[0] - neighbours[2]
    result = owned + prior[None, :] * coupling
    return (result[None, :arms], result[None, arms:])


def solution(mesh):
    finer = Mesh(mesh.devices.reshape(mesh.shape["day"], 4, 8), ("day", "row_0", "row_1"))
    return jax.shard_map(
        on_device,
        mesh=finer,
        in_specs=(
            P("day", ROW, None, None, None),
            P("day", ROW, None),
            P("day", ROW, None),
            P("day", None, ROW),
            P("day", None, ROW),
            P(ROW),
        ),
        out_specs=(P("day", None, ROW), P("day", None, ROW)),
        check_vma=False,
    )
```

profile of v0, /device:TPU:2, one launch (start us, length us, event | category | flops | bytes accessed | tf_op | source)
XLA Modules:
  0.0 209.9 jit_solution(5084960627540762023)
XLA Ops:
  7.2 0.9 constant_dynamic-update-slice_fusion.1
  8.1 0.9 constant_dynamic-update-slice_fusion
  9.1 30.9 %all_gather.6 = bf16[64,32,128]{2,1,0:T(8,128)(2,1)} all-gather(bf16[8,32,128]{2,1,0:T(8,128)(2,1)S(1)} %copy.30), channel_id=1, replica_groups=mesh['day'=8,'row_0'=4,'row_1'=8] {'row_1'}, dimensions={0}, use_global_device_ids=true | all-gather | bytes 589824 | tf_op jit(solution)/shard_map/all_gather | solution.py:45
  40.1 0.8 copy.34
  40.9 0.7 compare_select_fusion
  41.9 31.2 %all-gather.2.cloned.1.call-done = bf16[256,32,128]{2,1,0:T(8,128)(2,1)} async-done(((bf16[64,32,128]{2,1,0:T(8,128)(2,1)}), bf16[256,32,128]{2,1,0:T(8,128)(2,1)}) %all-gather.2.cloned.1.call-update) | async-done | bytes 2097168 | tf_op jit(solution)/shard_map/all_gather | solution.py:46
  73.1 2.8 %gather_fusion = bf16[384,32,128]{2,1,0:T(8,128)(2,1)S(1)} fusion(bf16[256,32,128]{2,1,0:T(8,128)(2,1)} %all-gather.2.cloned.1.call-done, s32[1024]{0:T(1024)S(1)} %pad_clamp_fusion), kind=kCustom, calls=%fused_computation | custom fusion | bytes 6292992 | tf_op jit(solution)/shard_map/gather | solution.py:51
  76.0 7.0 %fusion.13 = f32[24,32,128]{2,1,0:T(8,128)S(1)} fusion(bf16[24,16,32,128]{3,2,1,0:T(8,128)(2,1)S(1)} %bitcast.59, bf16[1,24,16,128,128]{4,3,2,1,0:T(8,128)(2,1)} %param.6), kind=kOutput, calls=%fused_computation.16 | convolution fusion | flops 402653184 | bytes 16121856 | tf_op jit(solution)/shard_map/tari,taki->tkr/dot_general | solution.py:53
  83.0 0.8 subtract_convert_fusion
  83.8 9.0 %fusion.10 = f32[24,16,32,128]{3,2,1,0:T(8,128)} fusion(bf16[1,24,16,128,128]{4,3,2,1,0:T(8,128)(2,1)} %param.6, bf16[24,16,128]{2,1,0:T(8,128)(2,1)S(1)} %fusion.19, bf16[24,16,128]{2,1,0:T(8,128)(2,1)S(1)} %get-tuple-element.10), kind=kOutput, calls=%fused_computation.15 | convolution fusion | flops 403046400 | bytes 19070976 | tf_op jit(solution)/shard_map/tari,tkr->taki/dot_general | solution.py:64
  92.8 7.2 %reshape.130 = f32[1,384,4096]{2,1,0:T(8,128)} reshape(f32[24,16,32,128]{3,2,1,0:T(8,128)} %fusion.10) | data formatting | bytes 12582912 | tf_op jit(solution)/shard_map/reshape | solution.py:65
  100.0 6.6 %copy.32 = f32[1,384,4096]{1,2,0:T(8,128)} copy(f32[1,384,4096]{2,1,0:T(8,128)} %reshape.130) | data formatting | bytes 12582912 | tf_op jit(solution)/shard_map/reshape | solution.py:65
  106.6 3.8 %reduce-precision_convert_fusion = (bf16[1,384,4096]{1,2,0:T(8,128)(2,1)S(1)}, bf16[1,384,4096]{1,2,0:T(8,128)(2,1)S(1)}) fusion(f32[1,384,4096]{1,2,0:T(8,128)} %copy.32), kind=kLoop, calls=%fused_computation.8 | loop fusion | flops 6291456 | bytes 12582912 | tf_op jit(solution)/shard_map/convert_element_type | solution.py:67
  110.3 2.4 %convolution_bitcast_fusion = f32[2,256,4096]{1,2,0:T(8,128)S(1)} fusion(bf16[1,384,4096]{1,2,0:T(8,128)(2,1)S(1)} %get-tuple-element.3, bf16[1,384,4096]{1,2,0:T(8,128)(2,1)S(1)} %get-tuple-element.2, s32[384]{0:T(512)S(1)} %eq.35, s32[256]{0:T(256)S(1)} %reshape.137), kind=kOutput, calls=%fused_computation.9 | convolution fusion | flops 1613856768 | bytes 14682624 | tf_op jit(solution)/shard_map/bp,jpc->jbc/dot_general | solution.py:73
  112.8 2.5 %slice_add_fusion = f32[1,256,4096]{1,2,0:T(8,128)} fusion(f32[2,256,4096]{1,2,0:T(8,128)S(1)} %convolution_bitcast_fusion), kind=kLoop, calls=%fused_computation.14 | loop fusion | flops 1048576 | bytes 12582912 | tf_op jit(solution)/shard_map/add | solution.py:76
  115.3 5.5 %copy.35 = f32[256,32,128]{2,1,0:T(8,128)} copy(f32[256,32,128]{0,2,1:T(8,128)} %bitcast.58) | data formatting | bytes 8388608 | tf_op jit(solution)/shard_map/add | solution.py:76
  120.8 55.5 %reduce-scatter.3.cloned.1.call-done = f32[32,32,128]{2,1,0:T(8,128)} async-done(((f32[256,32,128]{2,1,0:T(8,128)}), f32[32,32,128]{2,1,0:T(8,128)}) %reduce-scatter.3.cloned.1.call-update) | async-done | bytes 524304 | tf_op jit(solution)/shard_map/reduce_scatter | solution.py:77
  176.3 1.9 collective-permute-start
  178.3 3.6 %collective-permute-start.1 = (f32[1,32,1024]{2,1,0:T(8,128)S(1)}, f32[1,32,1024]{2,1,0:T(8,128)S(1)}, u32[]{:S(2)}, u32[]{:S(2)}) collective-permute-start(f32[1,32,1024]{2,1,0:T(8,128)S(1)} %get-tuple-element.6), channel_id=1, source_target_pairs={{32,0},{64,32},{96,64},{128,96},{160,128},{192,160},{224,192},{33,... | collective-permute-start | bytes 393224 | tf_op jit(solution)/shard_map/ppermute | solution.py:25
  181.9 0.7 collective-permute-done
  182.6 1.8 collective-permute-done.1
  184.4 17.3 %reduce-scatter.5.cloned.1.call-done = f32[8,32,128]{2,1,0:T(8,128)} async-done(((f32[32,32,128]{2,1,0:T(8,128)}), f32[8,32,128]{2,1,0:T(8,128)}) %reduce-scatter.5.cloned.1.call-update) | async-done | bytes 131088 | tf_op jit(solution)/shard_map/reduce_scatter | solution.py:78
  201.7 0.9 bitcast_add_fusion
  202.7 0.7 slice_bitcast_fusion
  (21 shorter events, 0.6 us)
Async XLA Ops:
  7.2 66.0 %all-gather.2.cloned.1.call-start = ((), (), s32[]{:S(2)}) async-start(), calls=%async_computation.2 | async-start | bytes 2621440 | tf_op jit(solution)/shard_map/all_gather | solution.py:46
  40.1 136.2 %reduce-scatter.3.cloned.1.call-start = ((), (), s32[]{:S(2)}) async-start(), calls=%async_computation.3 | async-start | bytes 4718592 | tf_op jit(solution)/shard_map/reduce_scatter | solution.py:77
  76.0 7.0 %copy-start.1 = (s32[1,24,128]{2,1,0:T(8,128)S(1)}, s32[1,24,128]{2,1,0:T(8,128)}, u32[]{:S(2)}) copy-start(s32[1,24,128]{2,1,0:T(8,128)} %param.8) | copy-start | bytes 36868
  120.8 81.0 %copy-start = (f32[1024]{0:T(1024)S(1)}, f32[1024]{0:T(1024)}, u32[]{:S(2)}) copy-start(f32[1024]{0:T(1024)} %param.11) | copy-start | bytes 12292
  120.8 80.9 %reduce-scatter.5.cloned.1.call-start = ((), (), s32[]{:S(2)}) async-start(), calls=%async_computation.4 | async-start | bytes 655360 | tf_op jit(solution)/shard_map/reduce_scatter | solution.py:78
  176.3 6.3 %collective-permute-start = (f32[1,32,1024]{2,1,0:T(8,128)S(1)}, f32[1,32,1024]{2,1,0:T(8,128)S(1)}, u32[]{:S(2)}, u32[]{:S(2)}) collective-permute-start(f32[1,32,1024]{2,1,0:T(8,128)S(1)} %get-tuple-element.6), channel_id=1, source_target_pairs={{0,32},{32,64},{64,96},{96,128},{128,160},{160,192},{192,224},{1,3... | collective-permute-start | bytes 393224 | tf_op jit(solution)/shard_map/ppermute | solution.py:23
  178.3 6.1 %collective-permute-start.1 = (f32[1,32,1024]{2,1,0:T(8,128)S(1)}, f32[1,32,1024]{2,1,0:T(8,128)S(1)}, u32[]{:S(2)}, u32[]{:S(2)}) collective-permute-start(f32[1,32,1024]{2,1,0:T(8,128)S(1)} %get-tuple-element.6), channel_id=1, source_target_pairs={{32,0},{64,32},{96,64},{128,96},{160,128},{192,160},{224,192},{33,... | collective-permute-start | bytes 393224 | tf_op jit(solution)/shard_map/ppermute | solution.py:25
Sparse Core Ops, SparseCore 0:
  40.2 32.8 all-gather.1
  120.9 55.3 reduce-scatter.2
  178.8 22.8 reduce-scatter.4
where the time goes:
time: 211 us; the launch traced here: 210 us
  waiting for transfers between devices  107 us (51%)
  blocking collectives  30.9 us (15%)
  local copies, waits for them, and re-layouts  23.8 us (11%)
  matrix products  18.5 us (9%)
  between operations  13.9 us (7%)
  other arithmetic  10.6 us (5%)
  starting transfers between devices  5.68 us (3%)
    reduce_scatter x1, waiting for transfers between devices, on_device(): lax.psum_scatter(partial_terms, 'row_1', scatter_dimension=0, tiled=True)  55.5 us
    all_gather x1, waiting for transfers between devices, on_device(): coef_table = lax.all_gather(coef_table, 'row_0', axis=0, tiled=True)  31.2 us
    all_gather x1, blocking collectives, on_device(): coef_table = lax.all_gather(by_block, 'row_1', axis=0, tiled=True)  30.9 us
    reduce_scatter x1, waiting for transfers between devices, on_device(): owned = lax.psum_scatter(owned, 'row_0', scatter_dimension=0, tiled=True)  17.3 us
    reshape x2, local copies, waits for them, and re-layouts, on_device(): contrib = contrib.reshape(-1, 2 * arms * width)  13.7 us
    dot_general x1, matrix products, on_device(): jnp.einsum('tari,tkr->taki', feats, both_low, preferred_element_type=jnp....  8.99 us
    dot_general x1, matrix products, on_device(): jnp.einsum('tari,taki->tkr', feats, selected, preferred_element_type=jnp....  7.03 us
    add x1, local copies, waits for them, and re-layouts, on_device(): partial_terms = (split[0] + split[1]).reshape(nblk, 2 * arms, width)  5.49 us
  transfers between devices with their start and end apart: 5, of which 5 were waited for; matrix products, arithmetic and copies ran while one was open for 1% of the time, Pallas kernels for 0%

commit v1 on v0

--- a/solution.py
+++ b/solution.py
@@ -3,6 +3,7 @@
 from jax import lax
 from jax.sharding import Mesh
 from jax.sharding import PartitionSpec as P
+from jax.lax import all_to_all, psum
 
 ROW = ("row_0", "row_1")
 
@@ -42,7 +43,9 @@
     coef_pair = jnp.concatenate([coef[0], direction[0]], axis=0).astype(jnp.bfloat16)
     local_blk = coef_pair.shape[1] // width
     by_block = coef_pair.reshape(2 * arms, local_blk, width).transpose(1, 0, 2)
-    coef_table = lax.all_gather(by_block, "row_1", axis=0, tiled=True)
+    coef_table = jnp.concatenate(
+        all_to_all(jnp.stack(psum(1, "row_1") * [by_block]), "row_1", 0, 0), axis=0
+    )
     coef_table = lax.all_gather(coef_table, "row_0", axis=0, tiled=True)
     nblk = coef_table.shape[0]
     both = jnp.concatenate([coef, direction], axis=1)

time: 211 us -> 202 us (0.957)
  blocking collectives: 30.9 us -> 25.9 us
  waiting for transfers between devices: 107 us -> 103 us
    all_gather x1 -> x0, blocking collectives: 30.9 us -> none  [on_device(): coef_table = lax.all_gather(by_block, 'row_1', axis=0, tiled=True)]
    all_to_all x0 -> x1, blocking collectives: none -> 25.9 us  [on_device(): all_to_all(jnp.stack(psum(1, 'row_1') * [by_block]), 'row_1', 0, 0)]
    all_gather x1, waiting for transfers between devices: 31.2 us -> 27.9 us  [on_device(): coef_table = lax.all_gather(coef_table, 'row_0', axis=0, tiled=True)]
where the time goes in v1:
time: 202 us
  waiting for transfers between devices  103 us (51%)
  blocking collectives  25.9 us (13%)
  local copies, waits for them, and re-layouts  23.9 us (12%)
  matrix products  18.5 us (9%)
  between operations  13.9 us (7%)
  other arithmetic  10.6 us (5%)
  starting transfers between devices  5.68 us (3%)
    reduce_scatter x1, waiting for transfers between devices, on_device(): lax.psum_scatter(partial_terms, 'row_1', scatter_dimension=0, tiled=True)  55.5 us
    all_gather x1, waiting for transfers between devices, on_device(): coef_table = lax.all_gather(coef_table, 'row_0', axis=0, tiled=True)  27.9 us
    all_to_all x1, blocking collectives, on_device(): all_to_all(jnp.stack(psum(1, 'row_1') * [by_block]), 'row_1', 0, 0)  25.9 us
    reduce_scatter x1, waiting for transfers between devices, on_device(): owned = lax.psum_scatter(owned, 'row_0', scatter_dimension=0, tiled=True)  17.3 us
    reshape x2, local copies, waits for them, and re-layouts, on_device(): contrib = contrib.reshape(-1, 2 * arms * width)  13.7 us
    dot_general x1, matrix products, on_device(): jnp.einsum('tari,tkr->taki', feats, both_low, preferred_element_type=jnp....  8.99 us
    dot_general x1, matrix products, on_device(): jnp.einsum('tari,taki->tkr', feats, selected, preferred_element_type=jnp....  7.03 us
    add x1, local copies, waits for them, and re-layouts, on_device(): partial_terms = (split[0] + split[1]).reshape(nblk, 2 * arms, width)  5.49 us
  transfers between devices with their start and end apart: 5, of which 5 were waited for; matrix products, arithmetic and copies ran while one was open for 1% of the time, Pallas kernels for 0%

profile of v1, /device:TPU:2, one launch (start us, length us, event | category | flops | bytes accessed | tf_op | source)
XLA Modules:
  0.0 201.7 jit_solution(490100856579530954)
XLA Ops:
  7.2 0.9 constant_dynamic-update-slice_fusion.1
  8.1 0.9 constant_dynamic-update-slice_fusion
  9.2 25.9 %all_to_all.5 = bf16[8,8,32,128]{3,2,1,0:T(8,128)(2,1)} all-to-all(bf16[8,8,32,128]{3,2,1,0:T(8,128)(2,1)S(1)} %stack.4), channel_id=1, replica_groups=mesh['day'=8,'row_0'=4,'row_1'=8] {'row_1'}, dimensions={0} | all-to-all | bytes 1048576 | tf_op jit(solution)/shard_map/all_to_all | solution.py:47
  35.2 0.8 copy.28
  35.9 0.7 compare_select_fusion
  37.0 27.9 %all-gather.2.cloned.1.call-done = bf16[256,32,128]{2,1,0:T(8,128)(2,1)} async-done(((bf16[64,32,128]{2,1,0:T(8,128)(2,1)}), bf16[256,32,128]{2,1,0:T(8,128)(2,1)}) %all-gather.2.cloned.1.call-update) | async-done | bytes 2097168 | tf_op jit(solution)/shard_map/all_gather | solution.py:49
  64.9 2.8 %gather_fusion = bf16[384,32,128]{2,1,0:T(8,128)(2,1)S(1)} fusion(bf16[256,32,128]{2,1,0:T(8,128)(2,1)} %all-gather.2.cloned.1.call-done, s32[1024]{0:T(1024)S(1)} %pad_clamp_fusion), kind=kCustom, calls=%fused_computation | custom fusion | bytes 6292992 | tf_op jit(solution)/shard_map/gather | solution.py:54
  67.8 7.0 %fusion.13 = f32[24,32,128]{2,1,0:T(8,128)S(1)} fusion(bf16[24,16,32,128]{3,2,1,0:T(8,128)(2,1)S(1)} %bitcast.60, bf16[1,24,16,128,128]{4,3,2,1,0:T(8,128)(2,1)} %param.6), kind=kOutput, calls=%fused_computation.16 | convolution fusion | flops 402653184 | bytes 16121856 | tf_op jit(solution)/shard_map/tari,taki->tkr/dot_general | solution.py:56
  74.8 0.8 subtract_convert_fusion
  75.7 9.0 %fusion.10 = f32[24,16,32,128]{3,2,1,0:T(8,128)} fusion(bf16[1,24,16,128,128]{4,3,2,1,0:T(8,128)(2,1)} %param.6, bf16[24,16,128]{2,1,0:T(8,128)(2,1)S(1)} %fusion.19, bf16[24,16,128]{2,1,0:T(8,128)(2,1)S(1)} %get-tuple-element.10), kind=kOutput, calls=%fused_computation.15 | convolution fusion | flops 403046400 | bytes 19070976 | tf_op jit(solution)/shard_map/tari,tkr->taki/dot_general | solution.py:67
  84.7 7.2 %reshape.136 = f32[1,384,4096]{2,1,0:T(8,128)} reshape(f32[24,16,32,128]{3,2,1,0:T(8,128)} %fusion.10) | data formatting | bytes 12582912 | tf_op jit(solution)/shard_map/reshape | solution.py:68
  91.8 6.6 %copy.26 = f32[1,384,4096]{1,2,0:T(8,128)} copy(f32[1,384,4096]{2,1,0:T(8,128)} %reshape.136) | data formatting | bytes 12582912 | tf_op jit(solution)/shard_map/reshape | solution.py:68
  98.4 3.8 %reduce-precision_convert_fusion = (bf16[1,384,4096]{1,2,0:T(8,128)(2,1)S(1)}, bf16[1,384,4096]{1,2,0:T(8,128)(2,1)S(1)}) fusion(f32[1,384,4096]{1,2,0:T(8,128)} %copy.26), kind=kLoop, calls=%fused_computation.8 | loop fusion | flops 6291456 | bytes 12582912 | tf_op jit(solution)/shard_map/convert_element_type | solution.py:70
  102.1 2.4 %convolution_bitcast_fusion = f32[2,256,4096]{1,2,0:T(8,128)S(1)} fusion(bf16[1,384,4096]{1,2,0:T(8,128)(2,1)S(1)} %get-tuple-element.3, bf16[1,384,4096]{1,2,0:T(8,128)(2,1)S(1)} %get-tuple-element.2, s32[384]{0:T(512)S(1)} %eq.35, s32[256]{0:T(256)S(1)} %reshape.143), kind=kOutput, calls=%fused_computation.9 | convolution fusion | flops 1613856768 | bytes 14682624 | tf_op jit(solution)/shard_map/bp,jpc->jbc/dot_general | solution.py:76
  104.6 2.5 %slice_add_fusion = f32[1,256,4096]{1,2,0:T(8,128)} fusion(f32[2,256,4096]{1,2,0:T(8,128)S(1)} %convolution_bitcast_fusion), kind=kLoop, calls=%fused_computation.14 | loop fusion | flops 1048576 | bytes 12582912 | tf_op jit(solution)/shard_map/add | solution.py:79
  107.1 5.5 %copy.29 = f32[256,32,128]{2,1,0:T(8,128)} copy(f32[256,32,128]{0,2,1:T(8,128)} %bitcast.59) | data formatting | bytes 8388608 | tf_op jit(solution)/shard_map/add | solution.py:79
  112.7 55.5 %reduce-scatter.3.cloned.1.call-done = f32[32,32,128]{2,1,0:T(8,128)} async-done(((f32[256,32,128]{2,1,0:T(8,128)}), f32[32,32,128]{2,1,0:T(8,128)}) %reduce-scatter.3.cloned.1.call-update) | async-done | bytes 524304 | tf_op jit(solution)/shard_map/reduce_scatter | solution.py:80
  168.2 1.9 collective-permute-start
  170.1 3.6 %collective-permute-start.1 = (f32[1,32,1024]{2,1,0:T(8,128)S(1)}, f32[1,32,1024]{2,1,0:T(8,128)S(1)}, u32[]{:S(2)}, u32[]{:S(2)}) collective-permute-start(f32[1,32,1024]{2,1,0:T(8,128)S(1)} %get-tuple-element.6), channel_id=1, source_target_pairs={{32,0},{64,32},{96,64},{128,96},{160,128},{192,160},{224,192},{33,... | collective-permute-start | bytes 393224 | tf_op jit(solution)/shard_map/ppermute | solution.py:26
  173.8 0.7 collective-permute-done
  174.5 1.8 collective-permute-done.1
  176.2 17.3 %reduce-scatter.5.cloned.1.call-done = f32[8,32,128]{2,1,0:T(8,128)} async-done(((f32[32,32,128]{2,1,0:T(8,128)}), f32[8,32,128]{2,1,0:T(8,128)}) %reduce-scatter.5.cloned.1.call-update) | async-done | bytes 131088 | tf_op jit(solution)/shard_map/reduce_scatter | solution.py:81
  193.5 0.9 bitcast_add_fusion
  194.5 0.7 slice_bitcast_fusion
  (22 shorter events, 0.7 us)
Async XLA Ops:
  7.2 57.8 %all-gather.2.cloned.1.call-start = ((), (), s32[]{:S(2)}) async-start(), calls=%async_computation.3 | async-start | bytes 2621440 | tf_op jit(solution)/shard_map/all_gather | solution.py:49
  35.1 133.0 %reduce-scatter.3.cloned.1.call-start = ((), (), s32[]{:S(2)}) async-start(), calls=%async_computation.4 | async-start | bytes 4718592 | tf_op jit(solution)/shard_map/reduce_scatter | solution.py:80
  67.8 7.0 %copy-start.1 = (s32[1,24,128]{2,1,0:T(8,128)S(1)}, s32[1,24,128]{2,1,0:T(8,128)}, u32[]{:S(2)}) copy-start(s32[1,24,128]{2,1,0:T(8,128)} %param.8) | copy-start | bytes 36868
  112.6 80.9 %copy-start = (f32[1024]{0:T(1024)S(1)}, f32[1024]{0:T(1024)}, u32[]{:S(2)}) copy-start(f32[1024]{0:T(1024)} %param.11) | copy-start | bytes 12292
  112.6 80.9 %reduce-scatter.5.cloned.1.call-start = ((), (), s32[]{:S(2)}) async-start(), calls=%async_computation.5 | async-start | bytes 655360 | tf_op jit(solution)/shard_map/reduce_scatter | solution.py:81
  168.2 6.3 %collective-permute-start = (f32[1,32,1024]{2,1,0:T(8,128)S(1)}, f32[1,32,1024]{2,1,0:T(8,128)S(1)}, u32[]{:S(2)}, u32[]{:S(2)}) collective-permute-start(f32[1,32,1024]{2,1,0:T(8,128)S(1)} %get-tuple-element.6), channel_id=1, source_target_pairs={{0,32},{32,64},{64,96},{96,128},{128,160},{160,192},{192,224},{1,3... | collective-permute-start | bytes 393224 | tf_op jit(solution)/shard_map/ppermute | solution.py:24
  170.1 6.1 %collective-permute-start.1 = (f32[1,32,1024]{2,1,0:T(8,128)S(1)}, f32[1,32,1024]{2,1,0:T(8,128)S(1)}, u32[]{:S(2)}, u32[]{:S(2)}) collective-permute-start(f32[1,32,1024]{2,1,0:T(8,128)S(1)} %get-tuple-element.6), channel_id=1, source_target_pairs={{32,0},{64,32},{96,64},{128,96},{160,128},{192,160},{224,192},{33,... | collective-permute-start | bytes 393224 | tf_op jit(solution)/shard_map/ppermute | solution.py:26
Sparse Core Ops, SparseCore 0:
  35.2 29.6 all-gather.1
  112.7 55.3 reduce-scatter.2
  170.7 22.8 reduce-scatter.4
